TPU v7x, 32 devices: a whole 2x2x4 slice. The times are simulated.
32 devices in a mesh: dp: 4 (over y, x), seq: 8 (over z, core).
Axes of the slice: x: 2, y: 2, z: 4, core: 2. Of those that a mesh axis runs over, the one named last changes fastest.
Arguments:
- queries: bfloat16 [6144, 2048], P(('dp', 'seq')), may hold values from -16 to 16
- keys: bfloat16 [6144, 2048], P(('dp', 'seq')), may hold values from -16 to 16
- values: bfloat16 [6144, 2048], P(('dp', 'seq')), may hold values from -6 to 6
- out_grad: bfloat16 [6144, 2048], P(('dp', 'seq')), may hold values from -6 to 6
- out_weight: bfloat16 [2048, 2048], P('dp'), may hold values from -0.125 to 0.125
- section_ids: int32 [6144], P(('dp', 'seq')), may hold values from 0 to 95, as said below
- masked: int32 [6144], P(('dp', 'seq')), may hold values from 0 to 1, as said below
Outputs:
- query_grad: bfloat16 [6144, 2048], P(('dp', 'seq'))
- key_grad: bfloat16 [6144, 2048], P(('dp', 'seq'))
- value_grad: bfloat16 [6144, 2048], P(('dp', 'seq'))
- weight_grad: float32 [2048, 2048], P('dp')
Inputs may be any that keep to these rules, and one draw needn't show every extreme that they name: `section_ids`: section numbers never fall along the tokens, are constant over each aligned block of 64 tokens, and no section spans two sequences of 1536 tokens. `masked`: the same for all tokens of a section.
All inputs are finite; a program needn't handle non-finite values.
Results may differ from a plain program's by a relative error of at most 0.015.
Values may be sent and summed in bfloat16 or wider, within the bound.
No kernel may reach another device: no remote copies, remote signals or barrier semaphores. Data moves between devices by JAX's collectives and lax.ppermute only.
A program may use at most 128 MiB of HBM per device.

v0:
```python
import jax
import jax.numpy as jnp
from jax import lax
from jax.sharding import PartitionSpec as P

HEAD_DIM = 128


def local(queries, keys, values, out_grad, out_weight, section_ids, masked):
    score_scale = HEAD_DIM ** (-0.5)
    attn_grad = lax.dot_general(
        out_grad,
        lax.all_gather(out_weight, "dp", axis=0, tiled=True),
        (((1,), (1,)), ((), ())),
        preferred_element_type=jnp.float32,
    ).astype(jnp.bfloat16)
    query_h, key_h, value_h = (
        lax.all_to_all(queries, "seq", split_axis=1, concat_axis=0, tiled=True),
        lax.all_to_all(keys, "seq", split_axis=1, concat_axis=0, tiled=True),
        lax.all_to_all(values, "seq", split_axis=1, concat_axis=0, tiled=True),
    )
    grad_h = lax.all_to_all(attn_grad, "seq", split_axis=1, concat_axis=0, tiled=True)
    n_seq = lax.axis_size("seq")
    code = section_ids * 2 + masked
    code_all = lax.all_to_all(
        jnp.broadcast_to(code[None], (n_seq,) + code.shape), "seq", 0, 0, tiled=True
    ).reshape(-1)
    sec_all = code_all // 2
    flag_all = code_all - 2 * sec_all
    grad_plane = lax.all_gather(out_grad, "dp", axis=0, tiled=True)
    seq_span = query_h.shape[0]
    width_here = query_h.shape[1]
    heads_here = width_here // HEAD_DIM
    block_rows = min(512, seq_span)
    num_blocks = seq_span // block_rows
    keys_head = key_h.reshape(seq_span, heads_here, HEAD_DIM)
    values_head = value_h.reshape(seq_span, heads_here, HEAD_DIM)
    visible_key = flag_all == 0

    def block_step(carried, block_item):
        key_acc, value_acc = carried
        query_blk, grad_blk, sec_blk = block_item
        scores = (
            jnp.einsum("qhd,khd->hqk", query_blk, keys_head, preferred_element_type=jnp.float32)
            * score_scale
        )
        allowed = visible_key[None, :] | (sec_blk[:, None] == sec_all[None, :])
        scores = jnp.where(allowed[None], scores, -1e30)
        row_max = jnp.max(scores, axis=2, keepdims=True)
        exp_scores = jnp.exp(scores - row_max)
        attn_probs = exp_scores / jnp.sum(exp_scores, axis=2, keepdims=True)
        probs_low = attn_probs.astype(jnp.bfloat16)
        out_blk = jnp.einsum(
            "hqk,khd->qhd", probs_low, values_head, preferred_element_type=jnp.float32
        ).astype(jnp.bfloat16)
        row_delta = jnp.sum(grad_blk.astype(jnp.float32) * out_blk.astype(jnp.float32), axis=2)
        prob_grad = jnp.einsum(
            "qhd,khd->hqk", grad_blk, values_head, preferred_element_type=jnp.float32
        )
        score_grad = (attn_probs * (prob_grad - row_delta.T[:, :, None])).astype(jnp.bfloat16)
        query_blk_grad = (
            jnp.einsum("hqk,khd->qhd", score_grad, keys_head, preferred_element_type=jnp.float32)
            * score_scale
        ).astype(jnp.bfloat16)
        key_acc = key_acc + jnp.einsum(
            "hqk,qhd->khd", score_grad, query_blk, preferred_element_type=jnp.float32
        )
        value_acc = value_acc + jnp.einsum(
            "hqk,qhd->khd", probs_low, grad_blk, preferred_element_type=jnp.float32
        )
        return ((key_acc, value_acc), (out_blk, query_blk_grad))

    scan_inputs = (
        query_h.reshape(num_blocks, block_rows, heads_here, HEAD_DIM),
        grad_h.reshape(num_blocks, block_rows, heads_here, HEAD_DIM),
        sec_all.reshape(num_blocks, block_rows),
    )
    zero_acc = jnp.zeros((seq_span, heads_here, HEAD_DIM), jnp.float32)
    (key_acc, value_acc), (out_blocks, query_blocks) = lax.scan(
        block_step, (zero_acc, zero_acc), scan_inputs
    )
    out_head = out_blocks.reshape(seq_span, width_here)
    query_grad_h = query_blocks.reshape(seq_span, width_here)
    key_grad_h = (key_acc * score_scale).astype(jnp.bfloat16).reshape(seq_span, width_here)
    value_grad_h = value_acc.astype(jnp.bfloat16).reshape(seq_span, width_here)
    attn_out, query_grad, key_grad, value_grad = (
        lax.all_to_all(out_head, "seq", split_axis=0, concat_axis=1, tiled=True),
        lax.all_to_all(query_grad_h, "seq", split_axis=0, concat_axis=1, tiled=True),
        lax.all_to_all(key_grad_h, "seq", split_axis=0, concat_axis=1, tiled=True),
        lax.all_to_all(value_grad_h, "seq", split_axis=0, concat_axis=1, tiled=True),
    )
    out_plane = lax.all_to_all(attn_out, "dp", split_axis=1, concat_axis=0, tiled=True)
    weight_grad = lax.psum(
        lax.dot_general(
            out_plane, grad_plane, (((0,), (0,)), ((), ())), preferred_element_type=jnp.float32
        ),
        "seq",
    )
    return (query_grad, key_grad, value_grad, weight_grad)


def solution(mesh):
    placed = (
        P(("dp", "seq"), None),
        P(("dp", "seq"), None),
        P(("dp", "seq"), None),
        P(("dp", "seq"), None),
        P("dp", None),
        P(("dp", "seq")),
        P(("dp", "seq")),
    )
    return jax.shard_map(
        local,
        mesh=mesh,
        in_specs=placed,
        out_specs=(
            P(("dp", "seq"), None),
            P(("dp", "seq"), None),
            P(("dp", "seq"), None),
            P("dp", None),
        ),
        check_vma=False,
    )
```

profile of v0, /device:TPU:0, one launch (start us, length us, event | category | flops | bytes accessed | tf_op | source)
XLA Modules:
  0.0 405.7 jit_solution(10119106563263983084)
XLA Ops:
  9.2 6.4 %all-to-all-start.1 = ((s32[8,1,192]{2,1,0:T(1,128)}), s32[8,1,192]{2,1,0:T(1,128)S(1)}, u32[]{:S(2)}, u32[]{:S(2)}) async-start(s32[8,1,192]{2,1,0:T(1,128)} %broadcast_in_dim.36), calls=%async_computation.1 | async-start | bytes 16384 | tf_op jit(solution)/shard_map/all_to_all | solution.py:25
  17.7 3.5 all-to-all-done.1
  21.2 3.6 all-to-all-start.2
  25.7 19.9 %all-to-all-done.2 = bf16[192,8,256]{2,0,1:T(8,128)(2,1)S(1)} async-done(((bf16[192,8,256]{2,0,1:T(8,128)(2,1)}), bf16[192,8,256]{2,0,1:T(8,128)(2,1)S(1)}, u32[]{:S(2)}, u32[]{:S(2)}) %all-to-all-start.2) | async-done | bytes 786464 | tf_op jit(solution)/shard_map/all_to_all | solution.py:19
  45.6 3.5 all-to-all-start.4
  50.1 19.9 %all-to-all-done.4 = bf16[192,8,256]{2,0,1:T(8,128)(2,1)S(1)} async-done(((bf16[192,8,256]{2,0,1:T(8,128)(2,1)}), bf16[192,8,256]{2,0,1:T(8,128)(2,1)S(1)}, u32[]{:S(2)}, u32[]{:S(2)}) %all-to-all-start.4) | async-done | bytes 786464 | tf_op jit(solution)/shard_map/all_to_all | solution.py:20
  70.1 3.5 all-to-all-start
  73.6 26.4 %all-gather.3.cloned.1.call-done = bf16[2048,2048]{1,0:T(8,128)(2,1)} async-done(((bf16[512,2048]{1,0:T(8,128)(2,1)}), bf16[2048,2048]{1,0:T(8,128)(2,1)}) %all-gather.3.cloned.1.call-update) | async-done | bytes 8388624 | tf_op jit(solution)/shard_map/all_gather | solution.py:13
  100.1 6.5 %convolution_convert_fusion.1 = bf16[192,2048]{1,0:T(8,128)(2,1)S(1)} fusion(bf16[192,2048]{1,0:T(8,128)(2,1)} %param.12, bf16[2048,2048]{1,0:T(8,128)(2,1)} %all-gather.3.cloned.1.call-done), kind=kOutput, calls=%fused_computation.31 | convolution fusion | flops 1611005952 | bytes 9961472 | tf_op jit(solution)/shard_map/dot_general | solution.py:11
  107.6 4.6 %all-to-all-start.3 = ((bf16[192,8,256]{2,0,1:T(8,128)(2,1)}), bf16[192,8,256]{2,0,1:T(8,128)(2,1)}, u32[]{:S(2)}, u32[]{:S(2)}) async-start(bf16[192,8,256]{2,0,1:T(8,128)(2,1)} %bitcast.76), calls=%async_computation.3 | async-start | bytes 1572864 | tf_op jit(solution)/shard_map/all_to_all | solution.py:22
  115.7 17.5 %all-to-all-done.3 = bf16[192,8,256]{2,0,1:T(8,128)(2,1)} async-done(((bf16[192,8,256]{2,0,1:T(8,128)(2,1)}), bf16[192,8,256]{2,0,1:T(8,128)(2,1)}, u32[]{:S(2)}, u32[]{:S(2)}) %all-to-all-start.3) | async-done | bytes 786464 | tf_op jit(solution)/shard_map/all_to_all | solution.py:22
  135.2 65.2 %while.17 = (s32[]{:T(128)}, f32[1536,2,128]{0,2,1:T(8,128)}, f32[1536,2,128]{0,2,1:T(8,128)}, bf16[3,512,2,128]{3,2,1,0:T(2,128)(2,1)}, bf16[3,512,2,128]{3,2,1...) while((s32[]{:T(128)}, f32[1536,2,128]{0,2,1:T(8,128)}, ...), condition=%wide.region_4.5_spmd.clone, body=%wide.region_0.4_spmd.clone.sunk | while | flops 2435711488 | bytes 120883744 | solution.py:79
  136.1 5.0 %fusion.54 = (f32[2,512]{1,0:T(2,128)S(1)}, f32[2,512,1536]{2,1,0:T(8,128)}) fusion(pred[512,1536]{1,0:T(8,128)(4,1)S(1)} %compare_or_fusion.2, bf16[1536,2,128]{2,0,1:T(8,128)(2,1)S(1)} %get-tuple-element.300, bf16[1,512,2,128]{3,2,1,0:T(2,128)(2,1)S(1)} %constant_dynamic-slice_fusion.8), kind=kOutput, calls=%fused_computation.53.clone.1 | convolution fusion | flops 408946176 | bytes 8130560 | tf_op jit(solution)/shard_map/while/body/eval_jaxpr/sub | solution.py:50
  141.1 3.8 fusion.55
  156.2 5.0 %fusion.54 = (f32[2,512]{1,0:T(2,128)S(1)}, f32[2,512,1536]{2,1,0:T(8,128)}) fusion(pred[512,1536]{1,0:T(8,128)(4,1)S(1)} %compare_or_fusion.2, bf16[1536,2,128]{2,0,1:T(8,128)(2,1)S(1)} %get-tuple-element.300, bf16[1,512,2,128]{3,2,1,0:T(2,128)(2,1)S(1)} %constant_dynamic-slice_fusion.8), kind=kOutput, calls=%fused_computation.53.clone.1 | convolution fusion | flops 408946176 | bytes 8130560 | tf_op jit(solution)/shard_map/while/body/eval_jaxpr/sub | solution.py:50
  161.2 3.8 fusion.55
  174.4 3.5 fusion.57
  178.7 5.0 %fusion.54 = (f32[2,512]{1,0:T(2,128)S(1)}, f32[2,512,1536]{2,1,0:T(8,128)}) fusion(pred[512,1536]{1,0:T(8,128)(4,1)S(1)} %compare_or_fusion.2, bf16[1536,2,128]{2,0,1:T(8,128)(2,1)S(1)} %get-tuple-element.300, bf16[1,512,2,128]{3,2,1,0:T(2,128)(2,1)S(1)} %constant_dynamic-slice_fusion.8), kind=kOutput, calls=%fused_computation.53.clone.1 | convolution fusion | flops 408946176 | bytes 8130560 | tf_op jit(solution)/shard_map/while/body/eval_jaxpr/sub | solution.py:50
  183.7 3.8 fusion.55
  203.7 3.8 all-to-all-start.8
  209.6 18.5 %all-to-all-done.8 = bf16[8,192,256]{2,1,0:T(8,128)(2,1)S(1)} async-done(((bf16[8,192,256]{2,1,0:T(8,128)(2,1)}), bf16[8,192,256]{2,1,0:T(8,128)(2,1)S(1)}, u32[]{:S(2)}, u32[]{:S(2)}) %all-to-all-start.8) | async-done | bytes 786464 | tf_op jit(solution)/shard_map/all_to_all | solution.py:87
  228.1 3.5 all-to-all-start.6
  233.6 18.9 %all-to-all-done.6 = bf16[8,192,256]{2,1,0:T(8,128)(2,1)S(1)} async-done(((bf16[8,192,256]{2,1,0:T(8,128)(2,1)}), bf16[8,192,256]{2,1,0:T(8,128)(2,1)S(1)}, u32[]{:S(2)}, u32[]{:S(2)}) %all-to-all-start.6) | async-done | bytes 786464 | tf_op jit(solution)/shard_map/all_to_all | solution.py:89
  252.5 3.5 all-to-all-start.9
  259.5 7.3 %all-to-all-done.9 = bf16[192,4,512]{2,0,1:T(8,128)(2,1)S(1)} async-done(((bf16[192,4,512]{2,0,1:T(8,128)(2,1)}), bf16[192,4,512]{2,0,1:T(8,128)(2,1)S(1)}, u32[]{:S(2)}, u32[]{:S(2)}) %all-to-all-start.9) | async-done | bytes 786464 | tf_op jit(solution)/shard_map/all_to_all | solution.py:92
  266.8 3.5 all-to-all-start.7
  270.5 5.7 %fusion.20 = f32[512,2048]{1,0:T(8,128)} fusion(bf16[768,512]{1,0:T(8,128)(2,1)S(1)} %bitcast.122, bf16[768,2048]{1,0:T(8,128)(2,1)} %all-gather.5.cloned.1.call-done), kind=kOutput, calls=%fused_computation.54 | convolution fusion | flops 1610612736 | bytes 8126464 | tf_op jit(solution)/shard_map/dot_general | solution.py:94
  278.7 16.3 %all-to-all-done.7 = bf16[8,192,256]{2,1,0:T(8,128)(2,1)S(1)} async-done(((bf16[8,192,256]{2,1,0:T(8,128)(2,1)}), bf16[8,192,256]{2,1,0:T(8,128)(2,1)S(1)}, u32[]{:S(2)}, u32[]{:S(2)}) %all-to-all-start.7) | async-done | bytes 786464 | tf_op jit(solution)/shard_map/all_to_all | solution.py:90
  295.0 3.5 all-to-all-start.5
  300.5 27.8 %all-to-all-done.5 = bf16[8,192,256]{2,1,0:T(8,128)(2,1)S(1)} async-done(((bf16[8,192,256]{2,1,0:T(8,128)(2,1)}), bf16[8,192,256]{2,1,0:T(8,128)(2,1)S(1)}, u32[]{:S(2)}, u32[]{:S(2)}) %all-to-all-start.5) | async-done | bytes 786464 | tf_op jit(solution)/shard_map/all_to_all | solution.py:88
  329.2 65.3 %all-reduce.2.cloned.1.call-done = f32[512,2048]{1,0:T(8,128)} async-done(((f32[512,2048]{1,0:T(8,128)}), f32[512,2048]{1,0:T(8,128)}) %all-reduce.2.cloned.1.call-update) | async-done | bytes 4194320 | tf_op jit(solution)/shard_map/psum | solution.py:93
  394.5 4.7 %copy.149 = f32[512,2048]{1,0:T(8,128)} copy(f32[512,2048]{1,0:T(8,128)} %all-reduce.2.cloned.1.call-done) | data formatting | bytes 8388608
  (162 shorter events, 63.6 us)
Async XLA Ops:
  7.2 17.6 %copy-start.11 = (bf16[192,2048]{1,0:T(8,128)(2,1)S(1)}, bf16[192,2048]{1,0:T(8,128)(2,1)}, u32[]{:S(2)}) copy-start(bf16[192,2048]{1,0:T(8,128)(2,1)} %param.11) | copy-start | bytes 2359300
  7.2 92.9 %all-gather.3.cloned.1.call-start = ((), (), s32[]{:S(2)}) async-start(), calls=%async_computation.10 | async-start | bytes 10485760 | tf_op jit(solution)/shard_map/all_gather | solution.py:13
  9.2 12.0 %all-to-all-start.1 = ((s32[8,1,192]{2,1,0:T(1,128)}), s32[8,1,192]{2,1,0:T(1,128)S(1)}, u32[]{:S(2)}, u32[]{:S(2)}) async-start(s32[8,1,192]{2,1,0:T(1,128)} %broadcast_in_dim.36), calls=%async_computation.1 | async-start | bytes 16384 | tf_op jit(solution)/shard_map/all_to_all | solution.py:25
  15.6 33.6 %copy-start.12 = (bf16[192,2048]{1,0:T(8,128)(2,1)S(1)}, bf16[192,2048]{1,0:T(8,128)(2,1)}, u32[]{:S(2)}) copy-start(bf16[192,2048]{1,0:T(8,128)(2,1)} %param.9) | copy-start | bytes 2359300
  21.2 24.5 %all-to-all-start.2 = ((bf16[192,8,256]{2,0,1:T(8,128)(2,1)}), bf16[192,8,256]{2,0,1:T(8,128)(2,1)S(1)}, u32[]{:S(2)}, u32[]{:S(2)}) async-start(bf16[192,8,256]{2,0,1:T(8,128)(2,1)} %bitcast.77), calls=%async_computation.2 | async-start | bytes 1572864 | tf_op jit(solution)/shard_map/all_to_all | solution.py:19
  45.6 24.4 %all-to-all-start.4 = ((bf16[192,8,256]{2,0,1:T(8,128)(2,1)}), bf16[192,8,256]{2,0,1:T(8,128)(2,1)S(1)}, u32[]{:S(2)}, u32[]{:S(2)}) async-start(bf16[192,8,256]{2,0,1:T(8,128)(2,1)} %bitcast.75), calls=%async_computation.4 | async-start | bytes 1572864 | tf_op jit(solution)/shard_map/all_to_all | solution.py:20
  70.1 37.5 %all-to-all-start = ((bf16[192,8,256]{2,0,1:T(8,128)(2,1)}), bf16[192,8,256]{2,0,1:T(8,128)(2,1)S(1)}, u32[]{:S(2)}, u32[]{:S(2)}) async-start(bf16[192,8,256]{2,0,1:T(8,128)(2,1)} %bitcast.78), calls=%async_computation | async-start | bytes 1572864 | tf_op jit(solution)/shard_map/all_to_all | solution.py:18
  107.6 25.7 %all-to-all-start.3 = ((bf16[192,8,256]{2,0,1:T(8,128)(2,1)}), bf16[192,8,256]{2,0,1:T(8,128)(2,1)}, u32[]{:S(2)}, u32[]{:S(2)}) async-start(bf16[192,8,256]{2,0,1:T(8,128)(2,1)} %bitcast.76), calls=%async_computation.3 | async-start | bytes 1572864 | tf_op jit(solution)/shard_map/all_to_all | solution.py:22
  112.2 158.3 %all-gather.5.cloned.1.call-start = ((), (), s32[]{:S(2)}) async-start(), calls=%async_computation.11 | async-start | bytes 3932160 | tf_op jit(solution)/shard_map/all_gather | solution.py:30
  135.2 5.8 %copy-start.3 = (bf16[1536,2,128]{2,0,1:T(8,128)(2,1)}, bf16[1536,2,128]{2,0,1:T(8,128)(2,1)S(1)}, u32[]{:S(2)}) copy-start(bf16[1536,2,128]{2,0,1:T(8,128)(2,1)S(1)} %get-tuple-element.300) | copy-start | bytes 2359300 | tf_op jit(solution)/shard_map/while
  135.3 5.8 %copy-start.7 = (bf16[3,512,2,128]{3,2,1,0:T(2,128)(2,1)}, bf16[3,512,2,128]{3,2,1,0:T(2,128)(2,1)S(1)}, u32[]{:S(2)}) copy-start(bf16[3,512,2,128]{3,2,1,0:T(2,128)(2,1)S(1)} %get-tuple-element.296) | copy-start | bytes 2359300 | tf_op jit(solution)/shard_map/while
  135.3 9.6 %copy-start.9 = (bf16[3,512,2,128]{3,2,1,0:T(2,128)(2,1)}, bf16[3,512,2,128]{3,2,1,0:T(2,128)(2,1)S(1)}, u32[]{:S(2)}) copy-start(bf16[3,512,2,128]{3,2,1,0:T(2,128)(2,1)S(1)} %get-tuple-element.301) | copy-start | bytes 2359300 | tf_op jit(solution)/shard_map/while
  141.1 5.1 %slice-start = ((s8[6291456]{0:T(1024)(128)(4,1)}), s8[4194304]{0:T(1024)(128)(4,1)S(1)}, s32[]{:S(2)}) async-start(s8[6291456]{0:T(1024)(128)(4,1)} %bitcast.119), calls=%async_computation.13 | async-start | bytes 8388608 | tf_op jit(solution)/shard_map/while
  141.1 4.0 copy-start.13
  141.1 5.1 %slice-start.1 = ((s8[6291456]{0:T(1024)(128)(4,1)}), s8[2097152]{0:T(1024)(128)(4,1)S(1)}, s32[]{:S(2)}) async-start(s8[6291456]{0:T(1024)(128)(4,1)} %bitcast.119), calls=%async_computation.14 | async-start | bytes 4194304 | tf_op jit(solution)/shard_map/while
  155.3 5.8 %copy-start.3 = (bf16[1536,2,128]{2,0,1:T(8,128)(2,1)}, bf16[1536,2,128]{2,0,1:T(8,128)(2,1)S(1)}, u32[]{:S(2)}) copy-start(bf16[1536,2,128]{2,0,1:T(8,128)(2,1)S(1)} %get-tuple-element.300) | copy-start | bytes 2359300 | tf_op jit(solution)/shard_map/while
  155.3 5.8 %copy-start.7 = (bf16[3,512,2,128]{3,2,1,0:T(2,128)(2,1)}, bf16[3,512,2,128]{3,2,1,0:T(2,128)(2,1)S(1)}, u32[]{:S(2)}) copy-start(bf16[3,512,2,128]{3,2,1,0:T(2,128)(2,1)S(1)} %get-tuple-element.296) | copy-start | bytes 2359300 | tf_op jit(solution)/shard_map/while
  155.3 9.6 %copy-start.9 = (bf16[3,512,2,128]{3,2,1,0:T(2,128)(2,1)}, bf16[3,512,2,128]{3,2,1,0:T(2,128)(2,1)S(1)}, u32[]{:S(2)}) copy-start(bf16[3,512,2,128]{3,2,1,0:T(2,128)(2,1)S(1)} %get-tuple-element.301) | copy-start | bytes 2359300 | tf_op jit(solution)/shard_map/while
  161.2 5.1 %slice-start = ((s8[6291456]{0:T(1024)(128)(4,1)}), s8[4194304]{0:T(1024)(128)(4,1)S(1)}, s32[]{:S(2)}) async-start(s8[6291456]{0:T(1024)(128)(4,1)} %bitcast.119), calls=%async_computation.13 | async-start | bytes 8388608 | tf_op jit(solution)/shard_map/while
  161.2 5.1 %slice-start.1 = ((s8[6291456]{0:T(1024)(128)(4,1)}), s8[2097152]{0:T(1024)(128)(4,1)S(1)}, s32[]{:S(2)}) async-start(s8[6291456]{0:T(1024)(128)(4,1)} %bitcast.119), calls=%async_computation.14 | async-start | bytes 4194304 | tf_op jit(solution)/shard_map/while
  177.9 5.8 %copy-start.3 = (bf16[1536,2,128]{2,0,1:T(8,128)(2,1)}, bf16[1536,2,128]{2,0,1:T(8,128)(2,1)S(1)}, u32[]{:S(2)}) copy-start(bf16[1536,2,128]{2,0,1:T(8,128)(2,1)S(1)} %get-tuple-element.300) | copy-start | bytes 2359300 | tf_op jit(solution)/shard_map/while
  177.9 5.8 %copy-start.7 = (bf16[3,512,2,128]{3,2,1,0:T(2,128)(2,1)}, bf16[3,512,2,128]{3,2,1,0:T(2,128)(2,1)S(1)}, u32[]{:S(2)}) copy-start(bf16[3,512,2,128]{3,2,1,0:T(2,128)(2,1)S(1)} %get-tuple-element.296) | copy-start | bytes 2359300 | tf_op jit(solution)/shard_map/while
  177.9 9.6 %copy-start.9 = (bf16[3,512,2,128]{3,2,1,0:T(2,128)(2,1)}, bf16[3,512,2,128]{3,2,1,0:T(2,128)(2,1)S(1)}, u32[]{:S(2)}) copy-start(bf16[3,512,2,128]{3,2,1,0:T(2,128)(2,1)S(1)} %get-tuple-element.301) | copy-start | bytes 2359300 | tf_op jit(solution)/shard_map/while
  183.7 5.1 %slice-start = ((s8[6291456]{0:T(1024)(128)(4,1)}), s8[4194304]{0:T(1024)(128)(4,1)S(1)}, s32[]{:S(2)}) async-start(s8[6291456]{0:T(1024)(128)(4,1)} %bitcast.119), calls=%async_computation.13 | async-start | bytes 8388608 | tf_op jit(solution)/shard_map/while
  183.7 5.1 %slice-start.1 = ((s8[6291456]{0:T(1024)(128)(4,1)}), s8[2097152]{0:T(1024)(128)(4,1)S(1)}, s32[]{:S(2)}) async-start(s8[6291456]{0:T(1024)(128)(4,1)} %bitcast.119), calls=%async_computation.14 | async-start | bytes 4194304 | tf_op jit(solution)/shard_map/while
  200.4 7.0 %copy-start.2 = (f32[1536,2,128]{0,2,1:T(8,128)S(1)}, f32[1536,2,128]{0,2,1:T(8,128)}, u32[]{:S(2)}) copy-start(f32[1536,2,128]{0,2,1:T(8,128)} %get-tuple-element.70) | copy-start | bytes 4718596
  203.7 24.4 %all-to-all-start.8 = ((bf16[8,192,256]{2,1,0:T(8,128)(2,1)}), bf16[8,192,256]{2,1,0:T(8,128)(2,1)S(1)}, u32[]{:S(2)}, u32[]{:S(2)}) async-start(bf16[8,192,256]{2,1,0:T(8,128)(2,1)} %all_to_all.145), calls=%async_computation.8 | async-start | bytes 1572864 | tf_op jit(solution)/shard_map/all_to_all | solution.py:87
  228.1 24.4 %all-to-all-start.6 = ((bf16[8,192,256]{2,1,0:T(8,128)(2,1)}), bf16[8,192,256]{2,1,0:T(8,128)(2,1)S(1)}, u32[]{:S(2)}, u32[]{:S(2)}) async-start(bf16[8,192,256]{2,1,0:T(8,128)(2,1)} %all_to_all.137), calls=%async_computation.6 | async-start | bytes 1572864 | tf_op jit(solution)/shard_map/all_to_all | solution.py:89
  252.5 14.3 %all-to-all-start.9 = ((bf16[192,4,512]{2,0,1:T(8,128)(2,1)}), bf16[192,4,512]{2,0,1:T(8,128)(2,1)S(1)}, u32[]{:S(2)}, u32[]{:S(2)}) async-start(bf16[192,4,512]{2,0,1:T(8,128)(2,1)} %copy.77), calls=%async_computation.9 | async-start | bytes 1572864 | tf_op jit(solution)/shard_map/all_to_all | solution.py:92
  266.8 28.1 %all-to-all-start.7 = ((bf16[8,192,256]{2,1,0:T(8,128)(2,1)}), bf16[8,192,256]{2,1,0:T(8,128)(2,1)S(1)}, u32[]{:S(2)}, u32[]{:S(2)}) async-start(bf16[8,192,256]{2,1,0:T(8,128)(2,1)} %all_to_all.141), calls=%async_computation.7 | async-start | bytes 1572864 | tf_op jit(solution)/shard_map/all_to_all | solution.py:90
  270.4 124.1 %all-reduce.2.cloned.1.call-start = ((), (), s32[]{:S(2)}) async-start(), calls=%async_computation.12 | async-start | bytes 8388608 | tf_op jit(solution)/shard_map/psum | solution.py:93
  295.0 33.3 %all-to-all-start.5 = ((bf16[8,192,256]{2,1,0:T(8,128)(2,1)}), bf16[8,192,256]{2,1,0:T(8,128)(2,1)S(1)}, u32[]{:S(2)}, u32[]{:S(2)}) async-start(bf16[8,192,256]{2,1,0:T(8,128)(2,1)} %all_to_all.133), calls=%async_computation.5 | async-start | bytes 1572864 | tf_op jit(solution)/shard_map/all_to_all | solution.py:88
  (24 other events, 69.1 us)
Sparse Core Ops, SparseCore 0:
  9.8 90.1 all-gather.2
  114.8 44.3 all-gather.4
  276.3 118.0 all-reduce.1
where the time goes:
time: 407 us; the launch traced here: 406 us
  waiting for transfers between devices  243 us (60%)
  matrix products  57.8 us (14%)
  starting transfers between devices  39.8 us (10%)
  local copies, waits for them, and re-layouts  35.5 us (9%)
  other arithmetic  15.4 us (4%)
  between operations  14 us (3%)
    psum x1, waiting for transfers between devices, local(): lax.psum(lax.dot_general(out_plane, grad_plane, (((0,), (0,)), ((), ())),...  65.3 us
    all_to_all x1, waiting for transfers between devices, local(): lax.all_to_all(query_grad_h, 'seq', split_axis=0, concat_axis=1, tiled=True)  27.8 us
    all_gather x1, waiting for transfers between devices, local(): lax.all_gather(out_weight, 'dp', axis=0, tiled=True)  26.4 us
    all_to_all x1, waiting for transfers between devices, local(): lax.all_to_all(keys, 'seq', split_axis=1, concat_axis=0, tiled=True)  19.9 us
    all_to_all x1, waiting for transfers between devices, local(): lax.all_to_all(values, 'seq', split_axis=1, concat_axis=0, tiled=True)  19.9 us
    all_to_all x1, waiting for transfers between devices, local(): lax.all_to_all(key_grad_h, 'seq', split_axis=0, concat_axis=1, tiled=True)  18.9 us
    all_to_all x1, waiting for transfers between devices, local(): lax.all_to_all(out_head, 'seq', split_axis=0, concat_axis=1, tiled=True)  18.5 us
    all_to_all x1, waiting for transfers between devices, local(): lax.all_to_all(attn_grad, 'seq', split_axis=1, concat_axis=0, tiled=True)  17.5 us
  transfers between devices with their start and end apart: 13, of which 11 were waited for; matrix products, arithmetic and copies ran while one was open for 23% of the time, Pallas kernels for 0%

commit v1 on v0

--- a/solution.py
+++ b/solution.py
@@ -90,11 +90,14 @@
         lax.all_to_all(value_grad_h, "seq", split_axis=0, concat_axis=1, tiled=True),
     )
     out_plane = lax.all_to_all(attn_out, "dp", split_axis=1, concat_axis=0, tiled=True)
-    weight_grad = lax.psum(
-        lax.dot_general(
-            out_plane, grad_plane, (((0,), (0,)), ((), ())), preferred_element_type=jnp.float32
+    weight_grad = jnp.sum(
+        lax.all_gather(
+            lax.dot_general(
+                out_plane, grad_plane, (((0,), (0,)), ((), ())), preferred_element_type=jnp.float32
+            ),
+            "seq",
         ),
-        "seq",
+        axis=0,
     )
     return (query_grad, key_grad, value_grad, weight_grad)
 

time: 407 us -> 611 us (1.50)
  waiting for transfers between devices: 243 us -> 383 us
  blocking collectives: 0 us -> 24.4 us
  local copies, waits for them, and re-layouts: 35.5 us -> 58.6 us
  other arithmetic: 15.4 us -> 32.5 us
  matrix products: 57.8 us -> 47.1 us
  starting transfers between devices: 39.8 us -> 49.4 us
    all_gather x0 -> x1, waiting for transfers between devices: none -> 180 us  [local(): lax.all_gather(lax.dot_general(out_plane, grad_plane, (((0,), (0,)), ((),...]
    psum x1 -> x0, waiting for transfers between devices: 65.3 us -> none  [local(): lax.psum(lax.dot_general(out_plane, grad_plane, (((0,), (0,)), ((), ())),...]
    all_to_all x1, waiting for transfers between devices: 16.3 us -> 44.3 us  [local(): lax.all_to_all(value_grad_h, 'seq', split_axis=0, concat_axis=1, tiled=True)]
    all_to_all x0 -> x1, blocking collectives: none -> 24.4 us  [local(): lax.all_to_all(out_head, 'seq', split_axis=0, concat_axis=1, tiled=True)]
    all_to_all x1, waiting for transfers between devices: 19.9 us -> 0.01 us  [local(): lax.all_to_all(values, 'seq', split_axis=1, concat_axis=0, tiled=True)]
    all_to_all x1, waiting for transfers between devices: 0.01 us -> 19.9 us  [local(): lax.all_to_all(queries, 'seq', split_axis=1, concat_axis=0, tiled=True)]
    all_to_all x1 -> x0, waiting for transfers between devices: 18.5 us -> none  [local(): lax.all_to_all(out_head, 'seq', split_axis=0, concat_axis=1, tiled=True)]
    all_to_all x1, waiting for transfers between devices: 18.9 us -> 36.4 us  [local(): lax.all_to_all(key_grad_h, 'seq', split_axis=0, concat_axis=1, tiled=True)]
  transfers between devices with their start and end apart: 13 -> 12, of which waited for: 11 -> 10; matrix products, arithmetic and copies ran while one was open for 23% -> 17% of each run, Pallas kernels for 0% -> 0%
where the time goes in v1:
time: 611 us; the launch traced here: 609 us
  waiting for transfers between devices  383 us (63%)
  local copies, waits for them, and re-layouts  58.6 us (10%)
  starting transfers between devices  49.4 us (8%)
  matrix products  47.1 us (8%)
  other arithmetic  32.5 us (5%)
  blocking collectives  24.4 us (4%)
  between operations  14 us (2%)
    all_gather x1, waiting for transfers between devices, local(): lax.all_gather(lax.dot_general(out_plane, grad_plane, (((0,), (0,)), ((),...  180 us
    all_to_all x1, waiting for transfers between devices, local(): lax.all_to_all(value_grad_h, 'seq', split_axis=0, concat_axis=1, tiled=True)  44.3 us
    all_to_all x1, waiting for transfers between devices, local(): lax.all_to_all(key_grad_h, 'seq', split_axis=0, concat_axis=1, tiled=True)  36.4 us
    all_to_all x1, waiting for transfers between devices, local(): lax.all_to_all(query_grad_h, 'seq', split_axis=0, concat_axis=1, tiled=True)  33.5 us
    all_gather x1, waiting for transfers between devices, local(): lax.all_gather(out_weight, 'dp', axis=0, tiled=True)  26.4 us
    all_to_all x1, blocking collectives, local(): lax.all_to_all(out_head, 'seq', split_axis=0, concat_axis=1, tiled=True)  24.4 us
    all_to_all x1, waiting for transfers between devices, local(): lax.all_to_all(keys, 'seq', split_axis=1, concat_axis=0, tiled=True)  19.9 us
    all_to_all x1, waiting for transfers between devices, local(): lax.all_to_all(queries, 'seq', split_axis=1, concat_axis=0, tiled=True)  19.9 us
  transfers between devices with their start and end apart: 12, of which 10 were waited for; matrix products, arithmetic and copies ran while one was open for 17% of the time, Pallas kernels for 0%

profile of v1, /device:TPU:0, one launch (start us, length us, event | category | flops | bytes accessed | tf_op | source)
XLA Modules:
  0.0 609.0 jit_solution(10747280087941520110)
XLA Ops:
  9.2 6.4 %all-to-all-start.1 = ((s32[8,1,192]{2,1,0:T(1,128)}), s32[8,1,192]{2,1,0:T(1,128)S(1)}, u32[]{:S(2)}, u32[]{:S(2)}) async-start(s32[8,1,192]{2,1,0:T(1,128)} %broadcast_in_dim.36), calls=%async_computation.1 | async-start | bytes 16384 | tf_op jit(solution)/shard_map/all_to_all | solution.py:25
  17.7 3.5 all-to-all-done.1
  21.2 3.6 all-to-all-start
  25.7 19.9 %all-to-all-done = bf16[192,8,256]{2,0,1:T(8,128)(2,1)S(1)} async-done(((bf16[192,8,256]{2,0,1:T(8,128)(2,1)}), bf16[192,8,256]{2,0,1:T(8,128)(2,1)S(1)}, u32[]{:S(2)}, u32[]{:S(2)}) %all-to-all-start) | async-done | bytes 786464 | tf_op jit(solution)/shard_map/all_to_all | solution.py:18
  45.6 3.5 all-to-all-start.2
  50.1 19.9 %all-to-all-done.2 = bf16[192,8,256]{2,0,1:T(8,128)(2,1)S(1)} async-done(((bf16[192,8,256]{2,0,1:T(8,128)(2,1)}), bf16[192,8,256]{2,0,1:T(8,128)(2,1)S(1)}, u32[]{:S(2)}, u32[]{:S(2)}) %all-to-all-start.2) | async-done | bytes 786464 | tf_op jit(solution)/shard_map/all_to_all | solution.py:19
  70.1 3.5 all-to-all-start.4
  73.6 26.4 %all-gather.5.cloned.1.call-done = bf16[2048,2048]{1,0:T(8,128)(2,1)} async-done(((bf16[512,2048]{1,0:T(8,128)(2,1)}), bf16[2048,2048]{1,0:T(8,128)(2,1)}) %all-gather.5.cloned.1.call-update) | async-done | bytes 8388624 | tf_op jit(solution)/shard_map/all_gather | solution.py:13
  100.1 6.3 %convolution_convert_fusion.1 = bf16[192,2048]{1,0:T(8,128)(2,1)S(1)} fusion(bf16[192,2048]{1,0:T(8,128)(2,1)S(1)} %copy-done.7, bf16[2048,2048]{1,0:T(8,128)(2,1)} %all-gather.5.cloned.1.call-done), kind=kOutput, calls=%fused_computation.31 | convolution fusion | flops 1611005952 | bytes 9961472 | tf_op jit(solution)/shard_map/dot_general | solution.py:11
  107.3 4.6 all-to-all-start.3
  126.3 6.6 %all-to-all-done.3 = bf16[192,8,256]{2,0,1:T(8,128)(2,1)} async-done(((bf16[192,8,256]{2,0,1:T(8,128)(2,1)}), bf16[192,8,256]{2,0,1:T(8,128)(2,1)}, u32[]{:S(2)}, u32[]{:S(2)}) %all-to-all-start.3) | async-done | bytes 786464 | tf_op jit(solution)/shard_map/all_to_all | solution.py:22
  135.7 63.9 %while.17 = (s32[]{:T(128)}, f32[1536,2,128]{0,2,1:T(8,128)S(1)}, f32[1536,2,128]{0,2,1:T(8,128)S(1)}, bf16[3,512,2,128]{3,2,1,0:T(2,128)(2,1)}, bf16[3,512,2,12...) while((s32[]{:T(128)}, f32[1536,2,128]{0,2,1:T(8,128)S(1)}, ...), condition=%wide.region_4.5_spmd.clone, body=%wide.region_0.4_spmd.clone.sunk | while | flops 2435711488 | bytes 78939944 | solution.py:79
  140.1 6.4 %fusion.54 = (f32[2,512]{1,0:T(2,128)S(1)}, f32[2,512,1536]{2,1,0:T(8,128)}) fusion(pred[512,1536]{1,0:T(8,128)(4,1)} %compare_or_fusion.2, bf16[1536,2,128]{2,0,1:T(8,128)(2,1)} %get-tuple-element.300, bf16[1,512,2,128]{3,2,1,0:T(2,128)(2,1)S(1)} %constant_dynamic-slice_fusion.8), kind=kOutput, calls=%fused_computation.53.clone.1 | convolution fusion | flops 408946176 | bytes 8130560 | tf_op jit(solution)/shard_map/while/body/eval_jaxpr/sub | solution.py:50
  146.5 3.8 fusion.55
  161.4 6.4 %fusion.54 = (f32[2,512]{1,0:T(2,128)S(1)}, f32[2,512,1536]{2,1,0:T(8,128)}) fusion(pred[512,1536]{1,0:T(8,128)(4,1)} %compare_or_fusion.2, bf16[1536,2,128]{2,0,1:T(8,128)(2,1)} %get-tuple-element.300, bf16[1,512,2,128]{3,2,1,0:T(2,128)(2,1)S(1)} %constant_dynamic-slice_fusion.8), kind=kOutput, calls=%fused_computation.53.clone.1 | convolution fusion | flops 408946176 | bytes 8130560 | tf_op jit(solution)/shard_map/while/body/eval_jaxpr/sub | solution.py:50
  167.8 3.8 fusion.55
  182.7 6.4 %fusion.54 = (f32[2,512]{1,0:T(2,128)S(1)}, f32[2,512,1536]{2,1,0:T(8,128)}) fusion(pred[512,1536]{1,0:T(8,128)(4,1)} %compare_or_fusion.2, bf16[1536,2,128]{2,0,1:T(8,128)(2,1)} %get-tuple-element.300, bf16[1,512,2,128]{3,2,1,0:T(2,128)(2,1)S(1)} %constant_dynamic-slice_fusion.8), kind=kOutput, calls=%fused_computation.53.clone.1 | convolution fusion | flops 408946176 | bytes 8130560 | tf_op jit(solution)/shard_map/while/body/eval_jaxpr/sub | solution.py:50
  189.1 3.8 fusion.55
  199.6 3.1 all_to_all.145
  202.7 24.4 %all_to_all.162 = bf16[8,192,256]{2,1,0:T(8,128)(2,1)S(1)} all-to-all(bf16[8,192,256]{2,1,0:T(8,128)(2,1)} %all_to_all.145), channel_id=1, replica_groups=mesh['dp'=4,'seq'=8] {'seq'}, dimensions={0} | all-to-all | bytes 1572864 | tf_op jit(solution)/shard_map/all_to_all | solution.py:87
  233.2 4.2 all-to-all-start.9
  237.7 10.5 %all-to-all-done.9 = bf16[192,4,512]{2,0,1:T(8,128)(2,1)} async-done(((bf16[192,4,512]{2,0,1:T(8,128)(2,1)}), bf16[192,4,512]{2,0,1:T(8,128)(2,1)}, u32[]{:S(2)}, u32[]{:S(2)}) %all-to-all-start.9) | async-done | bytes 786464 | tf_op jit(solution)/shard_map/all_to_all | solution.py:92
  248.2 6.0 fusion.20
  254.2 3.1 all_to_all.133
  257.4 4.2 all-to-all-start.5
  266.3 33.5 %all-to-all-done.5 = bf16[8,192,256]{2,1,0:T(8,128)(2,1)} async-done(((bf16[8,192,256]{2,1,0:T(8,128)(2,1)}), bf16[8,192,256]{2,1,0:T(8,128)(2,1)}, u32[]{:S(2)}, u32[]{:S(2)}) %all-to-all-start.5) | async-done | bytes 786464 | tf_op jit(solution)/shard_map/all_to_all | solution.py:88
  299.8 15.5 %all-to-all-start.6 = ((bf16[8,192,256]{2,1,0:T(8,128)(2,1)}), bf16[8,192,256]{2,1,0:T(8,128)(2,1)S(1)}, u32[]{:S(2)}, u32[]{:S(2)}) async-start(bf16[8,192,256]{2,1,0:T(8,128)(2,1)} %all_to_all.137), calls=%async_computation.6 | async-start | bytes 1572864 | tf_op jit(solution)/shard_map/all_to_all | solution.py:89
  319.9 36.4 %all-to-all-done.6 = bf16[8,192,256]{2,1,0:T(8,128)(2,1)S(1)} async-done(((bf16[8,192,256]{2,1,0:T(8,128)(2,1)}), bf16[8,192,256]{2,1,0:T(8,128)(2,1)S(1)}, u32[]{:S(2)}, u32[]{:S(2)}) %all-to-all-start.6) | async-done | bytes 786464 | tf_op jit(solution)/shard_map/all_to_all | solution.py:89
  356.3 3.5 all-to-all-start.7
  363.0 44.3 %all-to-all-done.7 = bf16[8,192,256]{2,1,0:T(8,128)(2,1)S(1)} async-done(((bf16[8,192,256]{2,1,0:T(8,128)(2,1)}), bf16[8,192,256]{2,1,0:T(8,128)(2,1)S(1)}, u32[]{:S(2)}, u32[]{:S(2)}) %all-to-all-start.7) | async-done | bytes 786464 | tf_op jit(solution)/shard_map/all_to_all | solution.py:90
  408.3 180.0 %all-gather.9.cloned.1.call-done = f32[4096,2048]{1,0:T(8,128)} async-done(((f32[512,2048]{1,0:T(8,128)}), f32[4096,2048]{1,0:T(8,128)}) %all-gather.9.cloned.1.call-update) | async-done | bytes 33554448 | tf_op jit(solution)/shard_map/all_gather | solution.py:94
  588.3 14.1 %reduce_sum.27 = f32[512,2048]{1,0:T(8,128)} reduce(f32[8,512,2048]{2,1,0:T(8,128)} %bitcast.122, f32[]{:T(128)} %constant.42.clone.1), dimensions={0}, to_apply=%region_5.6 | reduce | flops 7340032 | bytes 37748740 | tf_op jit(solution)/shard_map/reduce_sum | solution.py:93
  (117 shorter events, 77.0 us)
Async XLA Ops:
  7.2 17.6 %copy-start.5 = (bf16[192,2048]{1,0:T(8,128)(2,1)S(1)}, bf16[192,2048]{1,0:T(8,128)(2,1)}, u32[]{:S(2)}) copy-start(bf16[192,2048]{1,0:T(8,128)(2,1)} %param.10) | copy-start | bytes 2359300
  7.2 92.9 %all-gather.5.cloned.1.call-start = ((), (), s32[]{:S(2)}) async-start(), calls=%async_computation.10 | async-start | bytes 10485760 | tf_op jit(solution)/shard_map/all_gather | solution.py:13
  9.2 12.0 %all-to-all-start.1 = ((s32[8,1,192]{2,1,0:T(1,128)}), s32[8,1,192]{2,1,0:T(1,128)S(1)}, u32[]{:S(2)}, u32[]{:S(2)}) async-start(s32[8,1,192]{2,1,0:T(1,128)} %broadcast_in_dim.36), calls=%async_computation.1 | async-start | bytes 16384 | tf_op jit(solution)/shard_map/all_to_all | solution.py:25
  15.6 33.6 %copy-start.6 = (bf16[192,2048]{1,0:T(8,128)(2,1)S(1)}, bf16[192,2048]{1,0:T(8,128)(2,1)}, u32[]{:S(2)}) copy-start(bf16[192,2048]{1,0:T(8,128)(2,1)} %param.11) | copy-start | bytes 2359300
  21.2 24.5 %all-to-all-start = ((bf16[192,8,256]{2,0,1:T(8,128)(2,1)}), bf16[192,8,256]{2,0,1:T(8,128)(2,1)S(1)}, u32[]{:S(2)}, u32[]{:S(2)}) async-start(bf16[192,8,256]{2,0,1:T(8,128)(2,1)} %bitcast.79), calls=%async_computation | async-start | bytes 1572864 | tf_op jit(solution)/shard_map/all_to_all | solution.py:18
  24.8 75.3 %copy-start.7 = (bf16[192,2048]{1,0:T(8,128)(2,1)S(1)}, bf16[192,2048]{1,0:T(8,128)(2,1)}, u32[]{:S(2)}) copy-start(bf16[192,2048]{1,0:T(8,128)(2,1)} %param.12) | copy-start | bytes 2359300
  45.6 60.7 %copy-start.2 = (bf16[192,8,256]{2,0,1:T(8,128)(2,1)}, bf16[192,8,256]{2,0,1:T(8,128)(2,1)S(1)}, u32[]{:S(2)}) copy-start(bf16[192,8,256]{2,0,1:T(8,128)(2,1)S(1)} %all-to-all-done) | copy-start | bytes 2359300
  45.6 24.4 %all-to-all-start.2 = ((bf16[192,8,256]{2,0,1:T(8,128)(2,1)}), bf16[192,8,256]{2,0,1:T(8,128)(2,1)S(1)}, u32[]{:S(2)}, u32[]{:S(2)}) async-start(bf16[192,8,256]{2,0,1:T(8,128)(2,1)} %bitcast.78), calls=%async_computation.2 | async-start | bytes 1572864 | tf_op jit(solution)/shard_map/all_to_all | solution.py:19
  70.1 36.3 %copy-start.3 = (bf16[192,8,256]{2,0,1:T(8,128)(2,1)}, bf16[192,8,256]{2,0,1:T(8,128)(2,1)S(1)}, u32[]{:S(2)}) copy-start(bf16[192,8,256]{2,0,1:T(8,128)(2,1)S(1)} %all-to-all-done.2) | copy-start | bytes 2359300
  70.1 37.3 %all-to-all-start.4 = ((bf16[192,8,256]{2,0,1:T(8,128)(2,1)}), bf16[192,8,256]{2,0,1:T(8,128)(2,1)S(1)}, u32[]{:S(2)}, u32[]{:S(2)}) async-start(bf16[192,8,256]{2,0,1:T(8,128)(2,1)} %bitcast.76), calls=%async_computation.4 | async-start | bytes 1572864 | tf_op jit(solution)/shard_map/all_to_all | solution.py:20
  107.3 5.4 copy-start.4
  107.3 25.7 %all-to-all-start.3 = ((bf16[192,8,256]{2,0,1:T(8,128)(2,1)}), bf16[192,8,256]{2,0,1:T(8,128)(2,1)}, u32[]{:S(2)}, u32[]{:S(2)}) async-start(bf16[192,8,256]{2,0,1:T(8,128)(2,1)} %bitcast.77), calls=%async_computation.3 | async-start | bytes 1572864 | tf_op jit(solution)/shard_map/all_to_all | solution.py:22
  111.9 125.8 %all-gather.7.cloned.1.call-start = ((), (), s32[]{:S(2)}) async-start(), calls=%async_computation.11 | async-start | bytes 3932160 | tf_op jit(solution)/shard_map/all_gather | solution.py:30
  146.5 3.8 copy-start.1
  146.5 3.8 copy-start.8
  146.5 5.9 slice-start
  150.3 2.1 slice-start.1
  152.4 1.3 copy-start
  167.8 3.8 copy-start.1
  167.8 3.8 copy-start.8
  167.8 5.9 slice-start
  171.6 2.1 slice-start.1
  173.7 1.3 copy-start
  189.1 3.8 copy-start.1
  189.1 3.8 copy-start.8
  189.1 5.9 slice-start
  192.9 2.1 slice-start.1
  233.2 15.0 %all-to-all-start.9 = ((bf16[192,4,512]{2,0,1:T(8,128)(2,1)}), bf16[192,4,512]{2,0,1:T(8,128)(2,1)}, u32[]{:S(2)}, u32[]{:S(2)}) async-start(bf16[192,4,512]{2,0,1:T(8,128)(2,1)} %copy.77), calls=%async_computation.9 | async-start | bytes 1572864 | tf_op jit(solution)/shard_map/all_to_all | solution.py:92
  237.4 350.9 %all-gather.9.cloned.1.call-start = ((), (), s32[]{:S(2)}) async-start(), calls=%async_computation.12 | async-start | bytes 37748736 | tf_op jit(solution)/shard_map/all_gather | solution.py:94
  257.4 42.5 %all-to-all-start.5 = ((bf16[8,192,256]{2,1,0:T(8,128)(2,1)}), bf16[8,192,256]{2,1,0:T(8,128)(2,1)}, u32[]{:S(2)}, u32[]{:S(2)}) async-start(bf16[8,192,256]{2,1,0:T(8,128)(2,1)} %all_to_all.133), calls=%async_computation.5 | async-start | bytes 1572864 | tf_op jit(solution)/shard_map/all_to_all | solution.py:88
  299.8 56.5 %all-to-all-start.6 = ((bf16[8,192,256]{2,1,0:T(8,128)(2,1)}), bf16[8,192,256]{2,1,0:T(8,128)(2,1)S(1)}, u32[]{:S(2)}, u32[]{:S(2)}) async-start(bf16[8,192,256]{2,1,0:T(8,128)(2,1)} %all_to_all.137), calls=%async_computation.6 | async-start | bytes 1572864 | tf_op jit(solution)/shard_map/all_to_all | solution.py:89
  356.3 51.0 %all-to-all-start.7 = ((bf16[8,192,256]{2,1,0:T(8,128)(2,1)}), bf16[8,192,256]{2,1,0:T(8,128)(2,1)S(1)}, u32[]{:S(2)}, u32[]{:S(2)}) async-start(bf16[8,192,256]{2,1,0:T(8,128)(2,1)} %all_to_all.141), calls=%async_computation.7 | async-start | bytes 1572864 | tf_op jit(solution)/shard_map/all_to_all | solution.py:90
  (1 other events, 1.3 us)
Sparse Core Ops, SparseCore 0:
  9.8 90.1 all-gather.4
  114.6 44.3 all-gather.6
  254.3 333.9 all-gather.8
